TPU v7x, 256 devices: a whole 4x4x8 slice. The times are simulated.
256 devices in a mesh: expert: 16 (over y_hi, z), mp: 8 (over y_lo, x), batch: 2 (over core).
Axes of the slice: x: 4, y: 4 (y_hi: 2, y_lo: 2; y = y_hi * 2 + y_lo), z: 8, core: 2. Of those that a mesh axis runs over, the one named last changes fastest.
Arguments:
- tokens: bfloat16 [2, 2048, 2880], P('batch', 'expert', 'mp'), may hold values from -6 to 6
- segments: int32 [2, 2048], P('batch'), may hold values from 0 to 63, never falling along the last dimension, each value on 1 to 1024 neighbouring positions
- attn_gain: float32 [2880], replicated, may hold values from 0.6 to 9
- w_query: bfloat16 [2880, 4096], P('expert', 'mp'), may hold values from -0.109375 to 0.109375
- key_weight: bfloat16 [2880, 512], P('expert', 'mp'), may hold values from -0.109375 to 0.109375
- value_weight: bfloat16 [2880, 512], P('expert', 'mp'), may hold values from -0.109375 to 0.109375
- w_out: bfloat16 [4096, 2880], P('mp', 'expert'), may hold values from -0.09375 to 0.09375
- sink_head_logit: float32 [64], P('mp'), may hold values from -4 to 4
- moe_gain: float32 [2880], replicated, may hold values from 0.5 to 1.5
- expert_in: bfloat16 [16, 2, 2880, 2880], P('expert', None, None, 'mp'), may hold values from -0.3125 to 0.3125
- expert_down: bfloat16 [16, 2880, 2880], P('expert', 'mp'), may hold values from -0.01953125 to 0.01953125
- routes: int32 [2, 2048, 4], P('batch', 'expert'), may hold values from 0 to 15, all different within a row; in each aligned block of 128 rows (0 to 127, 128 to 255, ..., all dimensions but the last counted through in order) at most 48 rows name the same one
- route_weights: float32 [2, 2048, 4], P('batch', 'expert'), may hold values from 0.1 to 1
Outputs:
- hidden: bfloat16 [2, 2048, 2880], P('batch', 'expert', 'mp')
- key_cache: bfloat16 [2, 2048, 512], P('batch', 'expert', 'mp')
- value_cache: bfloat16 [2, 2048, 512], P('batch', 'expert', 'mp')
Inputs may be any that keep to these rules, and one draw needn't show every extreme that they name: Within each aligned block of 128 tokens of a micro-batch (the tokens of one index of expert), no expert is named by more than 48 routes; a token's routes name different experts. `segments`: segment numbers never fall along a micro-batch; one segment holds at most 1024 tokens.
All inputs are finite; a program needn't handle non-finite values.
Results may differ from a plain program's by a relative error of at most 0.024.
The roundings to bfloat16 on the way count: a program that leaves them out, or rounds other values in their place, can miss the bound.
Values may be sent and summed in bfloat16 or wider, within the bound.
No kernel may reach another device: no remote copies, remote signals or barrier semaphores. Data moves between devices by JAX's collectives and lax.ppermute only.
A program may use at most 64 MiB of HBM per device.

v0:
```python
import math
import jax
import jax.numpy as jnp
from jax import lax
from jax.sharding import PartitionSpec as P

HEAD_SIZE = 64
eps = 1e-05
rope_base = 150000.0
clamp_limit = 7.0
glu_alpha = 1.702


def rms_norm(row_block, gain):
    values = row_block.astype(jnp.float32)
    inv_scale = lax.rsqrt(jnp.mean(values * values, axis=-1, keepdims=True) + eps)
    return (values * inv_scale * gain).astype(jnp.bfloat16)


def apply_rotary(values, token_positions):
    half_dim = values.shape[-1] // 2
    inv_freq = jnp.power(
        rope_base, -2.0 * jnp.arange(half_dim, dtype=jnp.float32) / values.shape[-1]
    )
    rot_angle = token_positions.astype(jnp.float32)[:, None] * inv_freq[None, :]
    cosine = jnp.cos(rot_angle)[:, None, :]
    sine_val = jnp.sin(rot_angle)[:, None, :]
    first_half = values[..., :half_dim]
    second_half = values[..., half_dim:]
    return jnp.concatenate(
        [
            first_half * cosine - second_half * sine_val,
            second_half * cosine + first_half * sine_val,
        ],
        axis=-1,
    )


def expert_rows(row_block, w_in, w_down):
    gate_val = jnp.dot(row_block, w_in[0], preferred_element_type=jnp.float32)
    up_val = jnp.dot(row_block, w_in[1], preferred_element_type=jnp.float32)
    gate_val = jnp.minimum(gate_val, clamp_limit)
    up_val = jnp.clip(up_val, -clamp_limit, clamp_limit)
    activated = ((up_val + 1.0) * gate_val * jax.nn.sigmoid(glu_alpha * gate_val)).astype(
        jnp.bfloat16
    )
    return jnp.dot(activated, w_down, preferred_element_type=jnp.float32)


def shards(
    tokens,
    segments,
    attn_gain,
    w_query,
    key_weight,
    value_weight,
    w_out,
    sink_head_logit,
    moe_gain,
    expert_in,
    expert_down,
    routes,
    route_weights,
):
    local_rows = tokens[0]
    tok_count = local_rows.shape[0]
    expert_devs = lax.axis_size("expert")
    row_start = lax.axis_index("expert") * tok_count
    whole_rows = lax.all_gather(local_rows, "mp", axis=1, tiled=True)
    input_normalised = rms_norm(whole_rows, attn_gain)
    query_cols = w_query.shape[1]
    kv_cols = key_weight.shape[1]
    weight_parts = (
        lax.all_gather(w_query, "expert", axis=0, tiled=True),
        lax.all_gather(key_weight, "expert", axis=0, tiled=True),
        lax.all_gather(value_weight, "expert", axis=0, tiled=True),
    )
    query_raw, key_raw, value_raw = tuple(
        (
            jnp.dot(input_normalised, weight_part, preferred_element_type=jnp.float32)
            for weight_part in weight_parts
        )
    )
    token_positions = row_start + jnp.arange(tok_count, dtype=jnp.int32)
    query_by_head = query_cols // HEAD_SIZE
    kv_heads = kv_cols // HEAD_SIZE
    heads_per_group = query_by_head // kv_heads
    query_matrix = apply_rotary(
        query_raw.reshape(tok_count, query_by_head, HEAD_SIZE), token_positions
    ).astype(jnp.bfloat16)
    key_rotary = (
        apply_rotary(key_raw.reshape(tok_count, kv_heads, HEAD_SIZE), token_positions)
        .astype(jnp.bfloat16)
        .reshape(tok_count, kv_cols)
    )
    value_fresh = value_raw.astype(jnp.bfloat16)
    keys_all, values_all = (
        lax.all_gather(key_rotary, "expert", axis=0, tiled=True),
        lax.all_gather(value_fresh, "expert", axis=0, tiled=True),
    )
    seq_len = keys_all.shape[0]
    seg_all = segments[0]
    seg_local = lax.dynamic_slice_in_dim(seg_all, row_start, tok_count)
    row_total = heads_per_group * tok_count
    query_rows = (
        query_matrix.reshape(tok_count, kv_heads, heads_per_group, HEAD_SIZE)
        .transpose(1, 2, 0, 3)
        .reshape(kv_heads, row_total, HEAD_SIZE)
    )
    key_by_head = keys_all.reshape(seq_len, kv_heads, HEAD_SIZE).transpose(1, 0, 2)
    value_by_head = values_all.reshape(seq_len, kv_heads, HEAD_SIZE).transpose(1, 0, 2)
    row_pos = jnp.tile(token_positions, heads_per_group)
    row_seg = jnp.tile(seg_local, heads_per_group)
    sink_rows = jnp.repeat(sink_head_logit.reshape(kv_heads, heads_per_group), tok_count, axis=1)
    key_block = math.gcd(seq_len, 512)
    block_count = seq_len // key_block
    score_scale = HEAD_SIZE ** (-0.5)

    def block_scores(index):
        key_first = index * key_block
        key_part = lax.dynamic_slice_in_dim(key_by_head, key_first, key_block, 1)
        scores = (
            jnp.einsum("hrd,hkd->hrk", query_rows, key_part, preferred_element_type=jnp.float32)
            * score_scale
        )
        key_pos = key_first + jnp.arange(key_block, dtype=jnp.int32)
        key_seg = lax.dynamic_slice_in_dim(seg_all, key_first, key_block, 0)
        allowed = (key_pos[None, :] <= row_pos[:, None]) & (key_seg[None, :] == row_seg[:, None])
        return jnp.where(allowed[None], scores, -jnp.inf)

    def max_step(index, running):
        return jnp.maximum(running, jnp.max(block_scores(index), axis=-1))

    row_max = lax.fori_loop(0, block_count, max_step, sink_rows)

    def sum_step(index, carried):
        weighted, denom = carried
        probs = jnp.exp(block_scores(index) - row_max[..., None]).astype(jnp.bfloat16)
        value_part = lax.dynamic_slice_in_dim(value_by_head, index * key_block, key_block, 1)
        weighted = weighted + jnp.einsum(
            "hrk,hkd->hrd", probs, value_part, preferred_element_type=jnp.float32
        )
        denom = denom + jnp.sum(probs, axis=-1, dtype=jnp.float32)
        return (weighted, denom)

    init_pair = (
        jnp.zeros((kv_heads, row_total, HEAD_SIZE), jnp.float32),
        jnp.zeros((kv_heads, row_total), jnp.float32),
    )
    weighted, denom = lax.fori_loop(0, block_count, sum_step, init_pair)
    denom = denom + jnp.exp(sink_rows - row_max)
    mixed = (weighted / denom[..., None]).astype(jnp.bfloat16)
    mixed = (
        mixed.reshape(kv_heads, heads_per_group, tok_count, HEAD_SIZE)
        .transpose(2, 0, 1, 3)
        .reshape(tok_count, query_cols)
    )
    out_terms = jnp.dot(
        mixed,
        lax.all_gather(w_out, "expert", axis=1, tiled=True),
        preferred_element_type=jnp.float32,
    )
    attn_part = lax.psum_scatter(
        out_terms.astype(jnp.bfloat16), "mp", scatter_dimension=1, tiled=True
    ).astype(jnp.float32)
    first_out = (local_rows.astype(jnp.float32) + attn_part).astype(jnp.bfloat16)
    top_count = routes.shape[2]
    local_experts = expert_in.shape[0]
    expert_count = local_experts * expert_devs
    capacity = 3 * tok_count * top_count // (2 * expert_count)
    chosen = routes[0].reshape(tok_count * top_count)
    onehot = (chosen[:, None] == jnp.arange(expert_count, dtype=jnp.int32)[None, :]).astype(
        jnp.int32
    )
    ranks = jnp.sum((jnp.cumsum(onehot, axis=0) - onehot) * onehot, axis=1)
    target = chosen * capacity + ranks
    source_row = (
        jnp.full((expert_count * capacity,), tok_count, jnp.int32)
        .at[target]
        .set(jnp.arange(tok_count * top_count, dtype=jnp.int32) // top_count)
    )
    moe_whole = lax.all_gather(first_out, "mp", axis=1, tiled=True)
    moe_normed = rms_norm(moe_whole, moe_gain)
    padded = jnp.concatenate(
        [moe_normed, jnp.zeros((1, moe_normed.shape[1]), jnp.bfloat16)], axis=0
    )
    outgoing = padded[source_row].reshape(expert_count, capacity, padded.shape[1])
    arrived = lax.all_to_all(outgoing, "expert", split_axis=0, concat_axis=0, tiled=True)
    model_width = arrived.shape[2]
    grouped = arrived.reshape(expert_devs, local_experts, capacity, model_width)
    inputs = grouped[:, 0].reshape(expert_devs * capacity, model_width)
    partial_list = [
        expert_rows(inputs, expert_in[0], expert_down[0]).reshape(
            expert_devs, capacity, model_width
        )
    ]
    partials = jnp.stack(partial_list, axis=1).reshape(expert_count, capacity, model_width)
    expert_out = lax.psum_scatter(
        partials.astype(jnp.bfloat16), "mp", scatter_dimension=2, tiled=True
    )
    returned = lax.all_to_all(expert_out, "expert", split_axis=0, concat_axis=0, tiled=True)
    local_width = returned.shape[2]
    picked = returned.reshape(expert_count * capacity, local_width)[target].reshape(
        tok_count, top_count, local_width
    )
    moe_sum = jnp.sum(picked.astype(jnp.float32) * route_weights[0][..., None], axis=1)
    hidden = (first_out.astype(jnp.float32) + moe_sum).astype(jnp.bfloat16)
    return (hidden[None], key_rotary[None], value_fresh[None])


def solution(mesh):
    placed = (
        P("batch", "expert", "mp"),
        P("batch", None),
        P(),
        P("expert", "mp"),
        P("expert", "mp"),
        P("expert", "mp"),
        P("mp", "expert"),
        P("mp"),
        P(),
        P("expert", None, None, "mp"),
        P("expert", "mp", None),
        P("batch", "expert", None),
        P("batch", "expert", None),
    )
    return jax.shard_map(
        shards,
        mesh=mesh,
        in_specs=placed,
        out_specs=(
            P("batch", "expert", "mp"),
            P("batch", "expert", "mp"),
            P("batch", "expert", "mp"),
        ),
        check_vma=False,
    )
```

profile of v0, /device:TPU:1, one launch (start us, length us, event | category | flops | bytes accessed | tf_op | source)
XLA Modules:
  0.0 570.1 jit_solution(6893705568752840482)
XLA Ops:
  7.2 0.7 all-gather.8.cloned.1.call-update
  8.0 0.7 all-gather.10.cloned.1.call-update
  8.8 25.6 %all-gather = bf16[1,128,2880]{1,2,0:T(8,128)(2,1)S(1)} all-gather(bf16[1,128,360]{1,2,0:T(8,128)(2,1)} %param.17), channel_id=2, replica_groups=mesh['expert'=16,'mp'=8,'batch'=2] {'mp'}, dimensions={2}, use_global_device_ids=true | all-gather | bytes 829440 | tf_op jit(solution)/shard_map/all_gather | solution.py:69
  34.4 0.4 fusion.35
  34.8 40.1 %all-gather.1 = bf16[16,180,64]{1,2,0:T(8,128)(2,1)S(1)} all-gather(bf16[1,180,64]{1,2,0:T(8,128)(2,1)} %bitcast.211), channel_id=1, replica_groups=mesh['expert'=16,'mp'=8,'batch'=2] {'expert'}, dimensions={0}, use_global_device_ids=true | all-gather | bytes 391680 | tf_op jit(solution)/shard_map/all_gather | solution.py:75
  74.9 1.1 copy.73
  76.0 1.8 reshape.396
  77.8 0.8 multiply_cosine_fusion
  78.5 0.6 convolution_bitcast_fusion.1
  79.1 0.1 fusion.70
  79.3 31.8 %all_gather.26 = bf16[2048,64]{0,1:T(8,128)(2,1)S(1)} all-gather(bf16[128,64]{0,1:T(8,128)(2,1)S(1)} %pad_maximum_fusion), channel_id=1, replica_groups=mesh['expert'=16,'mp'=8,'batch'=2] {'expert'}, dimensions={0}, use_global_device_ids=true | all-gather | bytes 278528 | tf_op jit(solution)/shard_map/all_gather | solution.py:98
  111.1 1.0 copy.79
  112.2 33.1 %all-gather.3 = bf16[16,180,64]{1,2,0:T(8,128)(2,1)S(1)} all-gather(bf16[1,180,64]{1,2,0:T(8,128)(2,1)} %bitcast.212), channel_id=1, replica_groups=mesh['expert'=16,'mp'=8,'batch'=2] {'expert'}, dimensions={0}, use_global_device_ids=true | all-gather | bytes 391680 | tf_op jit(solution)/shard_map/all_gather | solution.py:76
  145.3 1.1 copy.78
  146.4 1.8 reshape.400
  148.2 1.3 convolution_convert_fusion.2
  149.5 35.5 %all_gather.29 = bf16[2048,64]{0,1:T(8,128)(2,1)} all-gather(bf16[128,64]{0,1:T(8,128)(2,1)S(1)} %convolution_convert_fusion.2), channel_id=1, replica_groups=mesh['expert'=16,'mp'=8,'batch'=2] {'expert'}, dimensions={0}, use_global_device_ids=true | all-gather | bytes 278528 | tf_op jit(solution)/shard_map/all_gather | solution.py:99
  185.1 4.4 reshape.398
  189.5 3.5 fusion.80
  193.1 0.9 copy.96
  194.0 7.0 %while.30 = (s32[]{:T(128)}, f32[1,1024]{1,0:T(1,128)S(1)}, s32[2048]{0:T(1024)S(1)}, bf16[1,2048,64]{2,1,0:T(8,128)(2,1)}, bf16[1,1024,64]{2,1,0:T(8,128)(2,1)}...) while((s32[]{:T(128)}, f32[1,1024]{1,0:T(1,128)S(1)}, ...), condition=%wide.region_3.4_spmd.clone, body=%wide.region_1.3_spmd.clone.sunk | while | flops 70255112 | bytes 437415 | solution.py:134
  194.1 1.6 fusion.101
  195.8 1.6 fusion.101
  197.6 1.6 fusion.101
  199.3 1.6 fusion.101
  201.0 12.7 %while.31 = (s32[]{:T(128)}, f32[1,1024,64]{1,2,0:T(8,128)S(1)}, f32[1,1024]{1,0:T(1,128)S(1)}, s32[2048]{0:T(1024)S(1)}, bf16[1,2048,64]{2,1,0:T(8,128)(2,1)}, ...) while((s32[]{:T(128)}, f32[1,1024,64]{1,2,0:T(8,128)S(1)}, ...), condition=%wide.region_6.7_spmd.clone, body=%wide.region_4.6_spmd.clone.sunk | while | flops 139068928 | bytes 3128526 | solution.py:150
  201.1 1.9 convert_reduce_fusion.2
  202.9 1.2 fusion.104
  204.2 1.9 convert_reduce_fusion.2
  206.1 1.2 fusion.104
  207.4 1.9 convert_reduce_fusion.2
  209.3 1.2 fusion.104
  210.6 1.9 convert_reduce_fusion.2
  212.4 1.2 fusion.104
  213.8 4.3 reshape.402
  218.1 3.7 convolution_convert_fusion.1
  222.4 1.2 reduce-window.6
  223.5 0.2 slice_reduce_fusion
  224.2 2.4 scatter_custom_fusion
  226.6 58.4 %reduce-scatter.10.cloned.1.call-done = bf16[128,360]{0,1:T(8,128)(2,1)} async-done(((bf16[128,2880]{0,1:T(8,128)(2,1)}), bf16[128,360]{0,1:T(8,128)(2,1)}) %reduce-scatter.10.cloned.1.call-update) | async-done | bytes 92176
  285.1 1.0 copy.83
  286.1 0.1 copy.84
  286.3 26.1 %all_gather.31 = bf16[128,2880]{0,1:T(8,128)(2,1)} all-gather(bf16[128,360]{0,1:T(8,128)(2,1)S(1)} %copy.84), channel_id=1, replica_groups=mesh['expert'=16,'mp'=8,'batch'=2] {'mp'}, dimensions={1}, use_global_device_ids=true | all-gather | bytes 829440 | tf_op jit(solution)/shard_map/all_gather | solution.py:182
  312.4 1.5 copy.85
  313.8 0.2 fusion.32
  314.1 0.2 fusion.34
  314.4 4.8 gather_fusion
  319.2 100.2 %all_to_all.10 = bf16[16,48,2880]{2,1,0:T(8,128)(2,1)S(1)} all-to-all(bf16[16,48,2880]{2,1,0:T(8,128)(2,1)} %bitcast.189), channel_id=1, replica_groups=mesh['expert'=16,'mp'=8,'batch'=2] {'expert'}, dimensions={0} | all-to-all | bytes 8847360 | tf_op jit(solution)/shard_map/all_to_all | solution.py:188
  419.4 3.5 fusion.38
  423.0 2.1 fusion.53
  425.0 0.3 copy.90
  425.3 4.1 convolution_convert_fusion
  429.5 14.6 %copy.94 = bf16[16,48,2880]{1,0,2:T(8,128)(2,1)} copy(bf16[16,48,2880]{2,1,0:T(8,128)(2,1)} %convolution_convert_fusion) | data formatting | bytes 8847360
  444.1 17.1 %reshape.409 = bf16[2880,768]{1,0:T(8,128)(2,1)} reshape(bf16[2880,16,48]{2,1,0:T(8,128)(2,1)} %bitcast.187) | data formatting | bytes 8847360
  461.2 64.7 %reduce-scatter.8.cloned.1.call-done = bf16[360,768]{1,0:T(8,128)(2,1)} async-done(((bf16[2880,768]{1,0:T(8,128)(2,1)}), bf16[360,768]{1,0:T(8,128)(2,1)}) %reduce-scatter.8.cloned.1.call-update) | async-done | bytes 552976
  525.9 3.6 reshape.410
  529.5 2.6 copy.95
  532.1 9.0 %all-to-all-start.1 = ((bf16[16,48,360]{2,1,0:T(8,128)(2,1)}), bf16[16,48,360]{2,1,0:T(8,128)(2,1)S(1)}, u32[]{:S(2)}, u32[]{:S(2)}) async-start(bf16[16,48,360]{2,1,0:T(8,128)(2,1)} %copy.95), calls=%async_computation.1 | async-start | bytes 1179648 | tf_op jit(solution)/shard_map/all_to_all | solution.py:201
  541.2 0.6 pad_maximum_fusion.1
  541.8 16.6 %all-to-all-done.1 = bf16[16,48,360]{2,1,0:T(8,128)(2,1)S(1)} async-done(((bf16[16,48,360]{2,1,0:T(8,128)(2,1)}), bf16[16,48,360]{2,1,0:T(8,128)(2,1)S(1)}, u32[]{:S(2)}, u32[]{:S(2)}) %all-to-all-start.1) | async-done | bytes 552992 | tf_op jit(solution)/shard_map/all_to_all | solution.py:201
  558.4 2.6 gather_fusion.1
  561.0 1.2 reshape.366
  562.2 0.5 multiply_reduce_fusion
  562.8 0.8 copy.92
  (110 shorter events, 2.4 us)
Async XLA Ops:
  7.2 418.2 %copy-start = (bf16[1,360,2880]{2,1,0:T(8,128)(2,1)S(1)}, bf16[1,360,2880]{2,1,0:T(8,128)(2,1)}, u32[]{:S(2)}) copy-start(bf16[1,360,2880]{2,1,0:T(8,128)(2,1)} %param.27) | copy-start | bytes 6220804
  7.2 177.9 %all-gather.8.cloned.1.call-start = ((), (), s32[]{:S(2)}) async-start(), calls=%async_computation.4 | async-start | bytes 3203072 | tf_op jit(solution)/shard_map/all_gather | solution.py:74
  7.9 205.9 %all-gather.10.cloned.1.call-start = ((), (), s32[]{:S(2)}) async-start(), calls=%async_computation.5 | async-start | bytes 3203072 | tf_op jit(solution)/shard_map/all_gather | solution.py:160
  8.7 69.9 %copy-start.10 = (f32[2880]{0:T(1024)S(1)}, f32[2880]{0:T(1024)}, u32[]{:S(2)}) copy-start(f32[2880]{0:T(1024)} %param.19) | copy-start | bytes 34564
  8.7 276.4 %reduce-scatter.10.cloned.1.call-start = ((), (), s32[]{:S(2)}) async-start(), calls=%async_computation.7 | async-start | bytes 829440
  34.8 43.7 %copy-start.12 = (f32[128]{0:T(128)}, f32[128]{0:T(128)S(1)}, u32[]{:S(2)}) copy-start(f32[128]{0:T(128)S(1)} %add_rsqrt_fusion.1) | copy-start | bytes 1540
  74.9 37.3 %copy-start.9 = (f32[8]{0:T(128)S(1)}, f32[8]{0:T(128)}, u32[]{:S(2)}) copy-start(f32[8]{0:T(128)} %param.24) | copy-start | bytes 100
  112.2 72.8 %copy-start.4 = (s32[1,2048]{1,0:T(1,128)S(1)}, s32[1,2048]{1,0:T(1,128)}, u32[]{:S(2)}) copy-start(s32[1,2048]{1,0:T(1,128)} %param.18) | copy-start | bytes 24580
  149.5 35.6 %copy-start.5 = (bf16[128,64]{0,1:T(8,128)(2,1)}, bf16[128,64]{0,1:T(8,128)(2,1)S(1)}, u32[]{:S(2)}) copy-start(bf16[128,64]{0,1:T(8,128)(2,1)S(1)} %convolution_convert_fusion.2) | copy-start | bytes 49156
  185.0 4.5 copy-start.11
  185.1 4.5 copy-start.13
  189.5 3.5 copy-start.2
  189.5 3.5 copy-start.3
  218.1 3.8 copy-start.1
  218.1 3.9 copy-start.7
  221.8 304.0 %reduce-scatter.8.cloned.1.call-start = ((), (), s32[]{:S(2)}) async-start(), calls=%async_computation.6 | async-start | bytes 4976640
  222.3 91.8 %copy-start.6 = (f32[2880]{0:T(1024)S(1)}, f32[2880]{0:T(1024)}, u32[]{:S(2)}) copy-start(f32[2880]{0:T(1024)} %param.25) | copy-start | bytes 34564
  319.2 103.7 %slice-start = ((s8[4239360]{0:T(1024)(128)(4,1)}), s8[4194304]{0:T(1024)(128)(4,1)S(1)}, s32[]{:S(2)}) async-start(s8[4239360]{0:T(1024)(128)(4,1)} %bitcast.219), calls=%async_computation.8 | async-start | bytes 8388608
  419.4 3.6 slice-start.1
  529.5 11.6 %copy-start.8 = (f32[1,128,4]{1,2,0:T(4,128)S(1)}, f32[1,128,4]{1,2,0:T(4,128)}, u32[]{:S(2)}) copy-start(f32[1,128,4]{1,2,0:T(4,128)} %param.29) | copy-start | bytes 6148
  532.1 26.4 %all-to-all-start.1 = ((bf16[16,48,360]{2,1,0:T(8,128)(2,1)}), bf16[16,48,360]{2,1,0:T(8,128)(2,1)S(1)}, u32[]{:S(2)}, u32[]{:S(2)}) async-start(bf16[16,48,360]{2,1,0:T(8,128)(2,1)} %copy.95), calls=%async_computation.1 | async-start | bytes 1179648 | tf_op jit(solution)/shard_map/all_to_all | solution.py:201
Sparse Core Ops, SparseCore 0:
  10.6 93.6 all-gather.7
  106.9 90.0 all-gather.9
  222.0 63.0 reduce-scatter.9
  461.3 64.5 reduce-scatter.7
where the time goes:
time: 572 us; the launch traced here: 570 us
  blocking collectives  292 us (51%)
  waiting for transfers between devices  141 us (25%)
  local copies, waits for them, and re-layouts  70.9 us (12%)
  matrix products  37.3 us (7%)
  between operations  14.2 us (2%)
  starting transfers between devices  9.14 us (2%)
    unnamed x6, waiting for transfers between devices  125 us
    all_to_all x1, blocking collectives, shards(): lax.all_to_all(outgoing, 'expert', split_axis=0, concat_axis=0, tiled=True)  100 us
    unnamed x47, local copies, waits for them, and re-layouts  53.2 us
    all_gather x1, blocking collectives, shards(): lax.all_gather(key_weight, 'expert', axis=0, tiled=True)  40.1 us
    all_gather x1, blocking collectives, shards(): lax.all_gather(value_fresh, 'expert', axis=0, tiled=True)  35.5 us
    all_gather x1, blocking collectives, shards(): lax.all_gather(value_weight, 'expert', axis=0, tiled=True)  33.1 us
    all_gather x1, blocking collectives, shards(): lax.all_gather(key_rotary, 'expert', axis=0, tiled=True)  31.8 us
    all_gather x1, blocking collectives, shards(): moe_whole = lax.all_gather(first_out, 'mp', axis=1, tiled=True)  26.1 us
  transfers between devices with their start and end apart: 5, of which 3 were waited for; matrix products, arithmetic and copies ran while one was open for 8% of the time, Pallas kernels for 0%

commit v1 on v0

--- a/solution.py
+++ b/solution.py
@@ -1,3 +1,4 @@
+import functools
 import math
 import jax
 import jax.numpy as jnp
@@ -9,6 +10,22 @@
 rope_base = 150000.0
 clamp_limit = 7.0
 glu_alpha = 1.702
+
+
+def close_the_racks(z_in, ax_name):
+    m_next = jnp.concatenate(
+        lax.all_to_all(
+            jnp.stack([z_in] * lax.axis_size(ax_name)),
+            axis_name=ax_name,
+            split_axis=0,
+            concat_axis=0,
+        ),
+        axis=0,
+    )
+    return m_next
+
+
+supply_all_shapes_over_axis = functools.partial(close_the_racks, ax_name="expert")
 
 
 def rms_norm(row_block, gain):
@@ -72,7 +89,7 @@
     kv_cols = key_weight.shape[1]
     weight_parts = (
         lax.all_gather(w_query, "expert", axis=0, tiled=True),
-        lax.all_gather(key_weight, "expert", axis=0, tiled=True),
+        supply_all_shapes_over_axis(key_weight),
         lax.all_gather(value_weight, "expert", axis=0, tiled=True),
     )
     query_raw, key_raw, value_raw = tuple(

time: 572 us -> 545 us (0.953)
  blocking collectives: 292 us -> 253 us
  starting transfers between devices: 9.14 us -> 21 us
    all_gather x1 -> x0, blocking collectives: 40.1 us -> none  [shards(): lax.all_gather(key_weight, 'expert', axis=0, tiled=True)]
    all_to_all x0 -> x1, starting transfers between devices: none -> 11.8 us  [close_the_racks(): lax.all_to_all(jnp.stack([z_in] * lax.axis_size(ax_name)), axis_name=ax_n...]
    unnamed x6, waiting for transfers between devices: 125 us -> 113 us
    all_gather x1, waiting for transfers between devices: 0.02 us -> 7.13 us  [shards(): lax.all_gather(w_out, 'expert', axis=1, tiled=True)]
    unnamed x47 -> x44, local copies, waits for them, and re-layouts: 53.2 us -> 52 us
  transfers between devices with their start and end apart: 5 -> 6, of which waited for: 3 -> 4; matrix products, arithmetic and copies ran while one was open for 8% -> 9% of each run, Pallas kernels for 0% -> 0%
where the time goes in v1:
time: 545 us; the launch traced here: 543 us
  blocking collectives  253 us (46%)
  waiting for transfers between devices  137 us (25%)
  local copies, waits for them, and re-layouts  72.5 us (13%)
  matrix products  38 us (7%)
  starting transfers between devices  21 us (4%)
  between operations  14.2 us (3%)
  other arithmetic  7.02 us (1%)
    unnamed x6, waiting for transfers between devices  113 us
    all_to_all x1, blocking collectives, shards(): lax.all_to_all(outgoing, 'expert', split_axis=0, concat_axis=0, tiled=True)  100 us
    unnamed x44, local copies, waits for them, and re-layouts  52 us
    all_gather x1, blocking collectives, shards(): lax.all_gather(value_weight, 'expert', axis=0, tiled=True)  37 us
    all_gather x1, blocking collectives, shards(): lax.all_gather(value_fresh, 'expert', axis=0, tiled=True)  33.2 us
    all_gather x1, blocking collectives, shards(): lax.all_gather(key_rotary, 'expert', axis=0, tiled=True)  31.2 us
    all_gather x1, blocking collectives, shards(): moe_whole = lax.all_gather(first_out, 'mp', axis=1, tiled=True)  26.1 us
    all_gather x1, blocking collectives, shards(): whole_rows = lax.all_gather(local_rows, 'mp', axis=1, tiled=True)  25.4 us
  transfers between devices with their start and end apart: 6, of which 4 were waited for; matrix products, arithmetic and copies ran while one was open for 9% of the time, Pallas kernels for 0%

profile of v1, /device:TPU:1, one launch (start us, length us, event | category | flops | bytes accessed | tf_op | source)
XLA Modules:
  0.0 542.7 jit_solution(5569524478276868250)
XLA Ops:
  7.2 0.7 all-gather.7.cloned.1.call-update
  7.9 1.6 stack.2
  9.5 11.8 %all-to-all-start = ((bf16[16,180,64]{1,2,0:T(8,128)(2,1)}), bf16[16,180,64]{1,2,0:T(8,128)(2,1)}, u32[]{:S(2)}, u32[]{:S(2)}) async-start(bf16[16,180,64]{1,2,0:T(8,128)(2,1)} %stack.2), calls=%async_computation | async-start | bytes 1048576 | tf_op jit(solution)/shard_map/all_to_all | solution.py:17
  21.4 0.7 all-gather.9.cloned.1.call-update
  22.2 0.6 multiply_power_fusion
  22.8 0.6 fusion.78
  23.4 25.4 %all-gather = bf16[1,128,2880]{1,2,0:T(8,128)(2,1)S(1)} all-gather(bf16[1,128,360]{1,2,0:T(8,128)(2,1)} %param.17), channel_id=2, replica_groups=mesh['expert'=16,'mp'=8,'batch'=2] {'mp'}, dimensions={2}, use_global_device_ids=true | all-gather | bytes 829440 | tf_op jit(solution)/shard_map/all_gather | solution.py:86
  48.7 0.4 fusion.35
  49.1 0.5 add_rsqrt_fusion.1
  49.7 37.0 %all-gather.2 = bf16[16,180,64]{1,2,0:T(8,128)(2,1)S(1)} all-gather(bf16[1,180,64]{1,2,0:T(8,128)(2,1)S(1)} %bitcast.210), channel_id=1, replica_groups=mesh['expert'=16,'mp'=8,'batch'=2] {'expert'}, dimensions={0}, use_global_device_ids=true | all-gather | bytes 391680 | tf_op jit(solution)/shard_map/all_gather | solution.py:93
  86.7 1.1 copy.77
  87.8 1.8 reshape.404
  89.6 1.3 convolution_convert_fusion.2
  90.9 0.6 copy-done.6
  91.5 33.2 %all_gather.25 = bf16[2048,64]{0,1:T(8,128)(2,1)} all-gather(bf16[128,64]{0,1:T(8,128)(2,1)S(1)} %convolution_convert_fusion.2), channel_id=1, replica_groups=mesh['expert'=16,'mp'=8,'batch'=2] {'expert'}, dimensions={0}, use_global_device_ids=true | all-gather | bytes 278528 | tf_op jit(solution)/shard_map/all_gather | solution.py:116
  124.8 0.8 multiply_cosine_fusion
  125.6 2.1 copy.72
  127.7 1.8 reshape.363
  129.5 1.3 convolution_bitcast_fusion.1
  130.8 0.8 fusion.70
  131.7 31.2 %all_gather.22 = bf16[2048,64]{0,1:T(8,128)(2,1)S(1)} all-gather(bf16[128,64]{0,1:T(8,128)(2,1)S(1)} %pad_maximum_fusion), channel_id=1, replica_groups=mesh['expert'=16,'mp'=8,'batch'=2] {'expert'}, dimensions={0}, use_global_device_ids=true | all-gather | bytes 278528 | tf_op jit(solution)/shard_map/all_gather | solution.py:115
  162.9 1.1 copy.78
  163.9 4.4 reshape.402
  168.3 3.5 fusion.80
  171.8 0.9 copy.95
  172.7 7.0 %while.30 = (s32[]{:T(128)}, f32[1,1024]{1,0:T(1,128)S(1)}, s32[2048]{0:T(1024)S(1)}, bf16[1,2048,64]{2,1,0:T(8,128)(2,1)}, bf16[1,1024,64]{2,1,0:T(8,128)(2,1)}...) while((s32[]{:T(128)}, f32[1,1024]{1,0:T(1,128)S(1)}, ...), condition=%wide.region_3.4_spmd.clone, body=%wide.region_1.3_spmd.clone.sunk | while | flops 70255112 | bytes 437415 | solution.py:151
  172.8 1.6 fusion.101
  174.5 1.6 fusion.101
  176.3 1.6 fusion.101
  178.0 1.6 fusion.101
  179.7 12.6 %while.31 = (s32[]{:T(128)}, f32[1,1024,64]{1,2,0:T(8,128)S(1)}, f32[1,1024]{1,0:T(1,128)S(1)}, s32[2048]{0:T(1024)S(1)}, bf16[1,2048,64]{2,1,0:T(8,128)(2,1)}, ...) while((s32[]{:T(128)}, f32[1,1024,64]{1,2,0:T(8,128)S(1)}, ...), condition=%wide.region_6.7_spmd.clone, body=%wide.region_4.6_spmd.clone.sunk | while | flops 139068928 | bytes 3128526 | solution.py:167
  179.8 1.9 convert_reduce_fusion.2
  181.7 1.2 fusion.104
  183.0 1.8 convert_reduce_fusion.2
  184.8 1.2 fusion.104
  186.1 1.9 convert_reduce_fusion.2
  188.0 1.2 fusion.104
  189.3 1.9 convert_reduce_fusion.2
  191.2 1.2 fusion.104
  192.5 7.1 %all-gather.9.cloned.1.call-done = bf16[16,180,512]{2,1,0:T(8,128)(2,1)} async-done(((bf16[1,180,512]{2,1,0:T(8,128)(2,1)}), bf16[16,180,512]{2,1,0:T(8,128)(2,1)}) %all-gather.9.cloned.1.call-update) | async-done | bytes 2949136 | tf_op jit(solution)/shard_map/all_gather | solution.py:177
  199.6 4.4 reshape.406
  204.0 3.7 convolution_convert_fusion.1
  208.2 1.2 reduce-window.6
  210.0 2.4 scatter_custom_fusion
  212.5 46.4 %reduce-scatter.10.cloned.1.call-done = bf16[128,360]{0,1:T(8,128)(2,1)} async-done(((bf16[128,2880]{0,1:T(8,128)(2,1)}), bf16[128,360]{0,1:T(8,128)(2,1)}) %reduce-scatter.10.cloned.1.call-update) | async-done | bytes 92176
  258.9 1.0 copy.82
  260.1 26.1 %all_gather.27 = bf16[128,2880]{0,1:T(8,128)(2,1)} all-gather(bf16[128,360]{0,1:T(8,128)(2,1)S(1)} %copy.83), channel_id=1, replica_groups=mesh['expert'=16,'mp'=8,'batch'=2] {'mp'}, dimensions={1}, use_global_device_ids=true | all-gather | bytes 829440 | tf_op jit(solution)/shard_map/all_gather | solution.py:199
  286.2 1.5 copy.84
  288.2 4.8 gather_fusion
  293.0 100.0 %all_to_all.15 = bf16[16,48,2880]{2,1,0:T(8,128)(2,1)S(1)} all-to-all(bf16[16,48,2880]{2,1,0:T(8,128)(2,1)} %bitcast.188), channel_id=1, replica_groups=mesh['expert'=16,'mp'=8,'batch'=2] {'expert'}, dimensions={0} | all-to-all | bytes 8847360 | tf_op jit(solution)/shard_map/all_to_all | solution.py:205
  393.0 3.5 fusion.38
  396.6 2.1 fusion.53
  399.0 4.1 convolution_convert_fusion
  403.1 14.6 %copy.93 = bf16[16,48,2880]{1,0,2:T(8,128)(2,1)} copy(bf16[16,48,2880]{2,1,0:T(8,128)(2,1)} %convolution_convert_fusion) | data formatting | bytes 8847360
  417.7 17.1 %reshape.413 = bf16[2880,768]{1,0:T(8,128)(2,1)} reshape(bf16[2880,16,48]{2,1,0:T(8,128)(2,1)} %bitcast.186) | data formatting | bytes 8847360
  434.8 65.3 %reduce-scatter.8.cloned.1.call-done = bf16[360,768]{1,0:T(8,128)(2,1)} async-done(((bf16[2880,768]{1,0:T(8,128)(2,1)}), bf16[360,768]{1,0:T(8,128)(2,1)}) %reduce-scatter.8.cloned.1.call-update) | async-done | bytes 552976
  500.1 3.6 reshape.414
  503.7 2.6 copy.94
  506.3 9.0 %all-to-all-start.2 = ((bf16[16,48,360]{2,1,0:T(8,128)(2,1)}), bf16[16,48,360]{2,1,0:T(8,128)(2,1)S(1)}, u32[]{:S(2)}, u32[]{:S(2)}) async-start(bf16[16,48,360]{2,1,0:T(8,128)(2,1)} %copy.94), calls=%async_computation.2 | async-start | bytes 1179648 | tf_op jit(solution)/shard_map/all_to_all | solution.py:218
  515.5 0.6 pad_maximum_fusion.1
  516.1 16.6 %all-to-all-done.2 = bf16[16,48,360]{2,1,0:T(8,128)(2,1)S(1)} async-done(((bf16[16,48,360]{2,1,0:T(8,128)(2,1)}), bf16[16,48,360]{2,1,0:T(8,128)(2,1)S(1)}, u32[]{:S(2)}, u32[]{:S(2)}) %all-to-all-start.2) | async-done | bytes 552992 | tf_op jit(solution)/shard_map/all_to_all | solution.py:218
  532.7 1.9 gather_fusion.1
  534.8 0.5 multiply_reduce_fusion
  535.4 0.8 copy.91
  (110 shorter events, 3.7 us)
Async XLA Ops:
  7.2 391.8 %copy-start = (bf16[1,360,2880]{2,1,0:T(8,128)(2,1)S(1)}, bf16[1,360,2880]{2,1,0:T(8,128)(2,1)}, u32[]{:S(2)}) copy-start(bf16[1,360,2880]{2,1,0:T(8,128)(2,1)} %param.27) | copy-start | bytes 6220804
  7.2 42.5 %copy-start.10 = (f32[8]{0:T(128)S(1)}, f32[8]{0:T(128)}, u32[]{:S(2)}) copy-start(f32[8]{0:T(128)} %param.24) | copy-start | bytes 100
  7.2 42.5 %copy-start.5 = (bf16[180,64]{0,1:T(8,128)(2,1)S(1)}, bf16[180,64]{0,1:T(8,128)(2,1)}, u32[]{:S(2)}) copy-start(bf16[180,64]{0,1:T(8,128)(2,1)} %param.22) | copy-start | bytes 69124
  7.2 156.7 %all-gather.7.cloned.1.call-start = ((), (), s32[]{:S(2)}) async-start(), calls=%async_computation.5 | async-start | bytes 3203072 | tf_op jit(solution)/shard_map/all_gather | solution.py:91
  9.5 116.1 %all-to-all-start = ((bf16[16,180,64]{1,2,0:T(8,128)(2,1)}), bf16[16,180,64]{1,2,0:T(8,128)(2,1)}, u32[]{:S(2)}, u32[]{:S(2)}) async-start(bf16[16,180,64]{1,2,0:T(8,128)(2,1)} %stack.2), calls=%async_computation | async-start | bytes 1048576 | tf_op jit(solution)/shard_map/all_to_all | solution.py:17
  21.3 178.3 %all-gather.9.cloned.1.call-start = ((), (), s32[]{:S(2)}) async-start(), calls=%async_computation.6 | async-start | bytes 3203072 | tf_op jit(solution)/shard_map/all_gather | solution.py:177
  22.1 67.5 %copy-start.2 = (s32[1,2048]{1,0:T(1,128)S(1)}, s32[1,2048]{1,0:T(1,128)}, u32[]{:S(2)}) copy-start(s32[1,2048]{1,0:T(1,128)} %param.18) | copy-start | bytes 24580
  22.1 236.8 %reduce-scatter.10.cloned.1.call-start = ((), (), s32[]{:S(2)}) async-start(), calls=%async_computation.8 | async-start | bytes 829440
  49.7 39.9 %copy-start.3 = (f32[8,128]{1,0:T(8,128)}, f32[8,128]{1,0:T(8,128)S(1)}, u32[]{:S(2)}) copy-start(f32[8,128]{1,0:T(8,128)S(1)} %broadcast_in_dim.74) | copy-start | bytes 12292
  90.9 0.6 copy-start.6
  163.9 4.4 copy-start.11
  163.9 4.4 copy-start.12
  179.7 12.7 %copy-start.4 = (f32[8,128]{1,0:T(8,128)S(1)}, f32[8,128]{1,0:T(8,128)}, u32[]{:S(2)}) copy-start(f32[8,128]{1,0:T(8,128)} %copy-done.3) | copy-start | bytes 12292
  204.0 3.8 copy-start.1
  204.0 3.9 copy-start.8
  207.7 292.4 %reduce-scatter.8.cloned.1.call-start = ((), (), s32[]{:S(2)}) async-start(), calls=%async_computation.7 | async-start | bytes 4976640
  208.1 79.8 %copy-start.7 = (f32[2880]{0:T(1024)S(1)}, f32[2880]{0:T(1024)}, u32[]{:S(2)}) copy-start(f32[2880]{0:T(1024)} %param.25) | copy-start | bytes 34564
  293.0 103.5 %slice-start = ((s8[4239360]{0:T(1024)(128)(4,1)}), s8[4194304]{0:T(1024)(128)(4,1)S(1)}, s32[]{:S(2)}) async-start(s8[4239360]{0:T(1024)(128)(4,1)} %bitcast.217), calls=%async_computation.9 | async-start | bytes 8388608
  393.0 3.6 slice-start.1
  503.7 11.6 %copy-start.9 = (f32[1,128,4]{1,2,0:T(4,128)S(1)}, f32[1,128,4]{1,2,0:T(4,128)}, u32[]{:S(2)}) copy-start(f32[1,128,4]{1,2,0:T(4,128)} %param.29) | copy-start | bytes 6148
  506.3 26.4 %all-to-all-start.2 = ((bf16[16,48,360]{2,1,0:T(8,128)(2,1)}), bf16[16,48,360]{2,1,0:T(8,128)(2,1)S(1)}, u32[]{:S(2)}, u32[]{:S(2)}) async-start(bf16[16,48,360]{2,1,0:T(8,128)(2,1)} %copy.94), calls=%async_computation.2 | async-start | bytes 1179648 | tf_op jit(solution)/shard_map/all_to_all | solution.py:218
Sparse Core Ops, SparseCore 0:
  10.6 97.1 all-gather.6
  110.4 89.1 all-gather.8
  207.8 51.0 reduce-scatter.9
  434.9 65.1 reduce-scatter.7
